TPU v7x, 128 devices: a whole 4x4x4 slice. The times are simulated.
128 devices in a mesh: grp: 8 (over z, core), dev: 16 (over y, x).
Axes of the slice: x: 4, y: 4, z: 4, core: 2. Of those that a mesh axis runs over, the one named last changes fastest.
Arguments:
- positions: float32 [3, 131072], P(None, ('grp', 'dev')), may hold values from -3 to 3
- velocities: float32 [3, 131072], P(None, ('grp', 'dev')), may hold values from -5 to 5
- accelerations: float32 [3, 131072], P(None, ('grp', 'dev')), may hold values from -3 to 3
- jerks: float32 [3, 131072], P(None, ('grp', 'dev')), may hold values from -3 to 3
- levels: int32 [131072], P(('grp', 'dev')), may hold values from 0 to 5
- counts: int32 [2, 128], replicated, may hold values from 1 to 256, 16384 in all within a row
- active_rows: int32 [2, 32768], P(None, ('grp', 'dev')), may hold values from 0 to 1023, as said below
Outputs:
- new_positions: float32 [3, 131072], P(None, ('grp', 'dev'))
- new_velocities: float32 [3, 131072], P(None, ('grp', 'dev'))
- new_accelerations: float32 [3, 131072], P(None, ('grp', 'dev'))
- new_jerks: float32 [3, 131072], P(None, ('grp', 'dev'))
Inputs may be any that keep to these rules, and one draw needn't show every extreme that they name: In each step the 128 counts sum to exactly 16384 and the largest of them is exactly 256. `active_rows`: for each step and device, the 256 entries of the device's slots are distinct indices of that device's own stars; only the first counts of them are live.
All inputs are finite; a program needn't handle non-finite values.
Results may differ from a plain program's by a relative error of at most 0.00022.
Values sent between devices are 32-bit elements; how exact they have to be, the bound alone decides.
No kernel may reach another device: no remote copies, remote signals or barrier semaphores. Data moves between devices by JAX's collectives and lax.ppermute only.
A program may use at most 128 MiB of HBM per device.

v0:
```python
import math
import jax
import jax.numpy as jnp
from jax import lax
from jax.sharding import PartitionSpec as P

tick_length = 1.0 / 128.0


def pair_block(targets, src_pos, src_vel, mass, soft_sq):
    gap_x = src_pos[0][None, :] - targets[0][:, None]
    gap_y = src_pos[1][None, :] - targets[1][:, None]
    gap_z = src_pos[2][None, :] - targets[2][:, None]
    drift_x = src_vel[0][None, :] - targets[3][:, None]
    drift_y = src_vel[1][None, :] - targets[4][:, None]
    drift_z = src_vel[2][None, :] - targets[5][:, None]
    squared = gap_x * gap_x + gap_y * gap_y + gap_z * gap_z + soft_sq
    inverse = lax.rsqrt(squared)
    weight = mass * inverse * inverse * inverse
    along = 3.0 * (gap_x * drift_x + gap_y * drift_y + gap_z * drift_z) * inverse * inverse
    return jnp.stack(
        [
            jnp.sum(weight * gap_x, axis=1),
            jnp.sum(weight * gap_y, axis=1),
            jnp.sum(weight * gap_z, axis=1),
            jnp.sum(weight * (drift_x - along * gap_x), axis=1),
            jnp.sum(weight * (drift_y - along * gap_y), axis=1),
            jnp.sum(weight * (drift_z - along * gap_z), axis=1),
        ]
    )


def block_terms(packed, src_pos, src_vel, mass, soft_sq):
    width, total = packed.shape
    block = math.gcd(total, 2048)
    grouped = packed.reshape(width, total // block, block).transpose(1, 0, 2)
    result = lax.map(lambda targets: pair_block(targets, src_pos, src_vel, mass, soft_sq), grouped)
    return result.transpose(1, 0, 2).reshape(width, total)


def predict(positions, velocities, accelerations, jerks, elapsed):
    span = elapsed[None, :]
    pred_pos = (
        positions
        + span * velocities
        + 0.5 * span * span * accelerations
        + span * span * span / 6.0 * jerks
    )
    pred_vel = velocities + span * accelerations + 0.5 * span * span * jerks
    return (pred_pos, pred_vel)


def correct(old_pos, old_vel, old_acc, old_jerk, force, jerk_new, span):
    span = span[None, :]
    new_vel = old_vel + 0.5 * span * (old_acc + force) + span * span / 12.0 * (old_jerk - jerk_new)
    new_pos = old_pos + 0.5 * span * (old_vel + new_vel) + span * span / 12.0 * (old_acc - force)
    return (new_pos, new_vel)


def shards(positions, velocities, accelerations, jerks, levels, counts, active_rows):
    devices_all = lax.axis_size("grp") * lax.axis_size("dev")
    my_rank = lax.axis_index("grp") * lax.axis_size("dev") + lax.axis_index("dev")
    star_dev = positions.shape[1]
    slot_cap = active_rows.shape[1]
    stars_all = star_dev * devices_all
    live_all = stars_all // 8
    mass = 1.0 / stars_all
    soft_sq = 0.0004 * (131072.0 / stars_all) ** (2.0 / 3.0)
    chunks = 4
    chunk = live_all // chunks
    last_time = -(jnp.left_shift(jnp.int32(1), levels) - 1).astype(jnp.float32) * tick_length
    for step in range(active_rows.shape[0]):
        now = (step + 1) * tick_length
        pred_pos, pred_vel = predict(positions, velocities, accelerations, jerks, now - last_time)
        rows = active_rows[step]
        targets = jnp.concatenate([pred_pos[:, rows], pred_vel[:, rows]], axis=0)
        step_counts = counts[step]
        own_count = step_counts[my_rank]
        inclusive = jnp.cumsum(step_counts).astype(jnp.int32)
        first = inclusive - step_counts
        place = jnp.arange(live_all, dtype=jnp.int32)
        owner = jnp.sum((inclusive[None, :] <= place[:, None]).astype(jnp.int32), axis=1)
        owner = jnp.minimum(owner, devices_all - 1)
        slot = owner * slot_cap + place - first[owner]
        gathered = lax.all_gather(targets[None], ("grp", "dev"), axis=0, tiled=True)
        flat = gathered.transpose(1, 0, 2).reshape(6, devices_all * slot_cap)
        compact = flat[:, slot]
        parts = []
        summed = None
        for c in range(chunks):
            piece = compact[:, c * chunk : (c + 1) * chunk]
            terms = block_terms(piece, pred_pos, pred_vel, mass, soft_sq)
            if summed is not None:
                terms, summed = lax.optimization_barrier((terms, summed))
                parts.append(summed)
            summed = lax.psum(terms, ("grp", "dev"))
        parts.append(summed)
        parts.append(jnp.zeros((6, slot_cap), jnp.float32))
        totals = jnp.concatenate(parts, axis=1)
        own = lax.dynamic_slice_in_dim(totals, first[my_rank], slot_cap, 1)
        span = now - last_time[rows]
        new_pos, new_vel = correct(
            positions[:, rows],
            velocities[:, rows],
            accelerations[:, rows],
            jerks[:, rows],
            own[:3],
            own[3:],
            span,
        )
        live = jnp.arange(slot_cap, dtype=jnp.int32) < own_count
        target = jnp.where(live, rows, star_dev)
        positions = positions.at[:, target].set(new_pos, mode="drop")
        velocities = velocities.at[:, target].set(new_vel, mode="drop")
        accelerations = accelerations.at[:, target].set(own[:3], mode="drop")
        jerks = jerks.at[:, target].set(own[3:], mode="drop")
        last_time = last_time.at[target].set(now, mode="drop")
    return (positions, velocities, accelerations, jerks)


def solution(mesh):
    placed = (
        P(None, ("grp", "dev")),
        P(None, ("grp", "dev")),
        P(None, ("grp", "dev")),
        P(None, ("grp", "dev")),
        P(("grp", "dev")),
        P(),
        P(None, ("grp", "dev")),
    )
    return jax.shard_map(
        shards,
        mesh=mesh,
        in_specs=placed,
        out_specs=(
            P(None, ("grp", "dev")),
            P(None, ("grp", "dev")),
            P(None, ("grp", "dev")),
            P(None, ("grp", "dev")),
        ),
        check_vma=False,
    )
```

profile of v0, /device:TPU:1, one launch (start us, length us, event | category | flops | bytes accessed | tf_op | source)
XLA Modules:
  0.0 1731.8 jit_solution(9103468403013295511)
XLA Ops:
  8.6 2.6 compare_select_fusion.4
  14.8 63.9 %all-gather.2 = f32[128,6,256]{2,1,0:T(8,128)S(1)} all-gather(f32[1,6,256]{2,1,0:T(8,128)S(1)} %maximum_bitcast_fusion), channel_id=2, replica_groups=mesh['grp'=8,'dev'=16] {'grp','dev'}, dimensions={0}, use_global_device_ids=true | all-gather | bytes 792576 | tf_op jit(solution)/shard_map/all_gather | solution.py:85
  78.7 8.4 copy.253
  87.8 2.3 convert_reduce_fusion.1
  90.3 97.2 %gather_fusion.6 = s32[16384]{0:T(1024)S(1)} fusion(s32[128]{0:T(128)S(1)} %get-tuple-element.734, s32[16384]{0:T(1024)S(1)} %broadcast_clamp_fusion.3), kind=kCustom, calls=%fused_computation.6 | custom fusion | bytes 196608 | tf_op jit(solution)/shard_map/gather | solution.py:84
  187.7 60.2 %gather_fusion.7 = f32[16384,6]{1,0:T(8,128)} fusion(f32[6,32768]{0,1:T(8,128)} %bitcast.632, s32[16384]{0:T(1024)S(1)} %broadcast_clamp_fusion.1), kind=kCustom, calls=%fused_computation.7 | custom fusion | bytes 851968 | tf_op jit(solution)/shard_map/gather | solution.py:87
  247.9 6.2 fusion.167
  254.0 2.2 copy.256
  256.3 32.8 %while.81 = (s32[]{:T(128)}, f32[2,6,2048]{2,1,0:T(8,128)S(1)}, f32[3,1024]{1,0:T(4,128)S(1)}, f32[2,6,2048]{2,1,0:T(8,128)S(1)}, f32[3,1024]{1,0:T(4,128)S(1)},...) while((s32[]{:T(128)}, f32[2,6,2048]{2,1,0:T(8,128)S(1)}, ...), condition=%wide.region_17.18_spmd, body=%wide.region_10.17_spmd.sunk | while | flops 85970952 | bytes 499925 | solution.py:37
  256.4 16.2 fusion.187
  272.8 16.2 fusion.187
  290.1 2.3 convert_reduce_fusion
  292.5 2.2 copy.255
  294.7 32.8 %while.80 = (s32[]{:T(128)}, f32[2,6,2048]{2,1,0:T(8,128)S(1)}, f32[3,1024]{1,0:T(4,128)S(1)}, f32[2,6,2048]{2,1,0:T(8,128)S(1)}, f32[3,1024]{1,0:T(4,128)S(1)},...) while((s32[]{:T(128)}, f32[2,6,2048]{2,1,0:T(8,128)S(1)}, ...), condition=%wide.region_9.10_spmd, body=%wide.region_2.9_spmd.sunk | while | flops 85970952 | bytes 499925 | solution.py:37
  294.8 16.2 fusion.185
  311.2 16.2 fusion.185
  327.5 2.3 copy.257
  329.8 32.8 %while.82 = (s32[]{:T(128)}, f32[2,6,2048]{2,1,0:T(8,128)S(1)}, f32[3,1024]{1,0:T(4,128)S(1)}, f32[2,6,2048]{2,1,0:T(8,128)S(1)}, f32[3,1024]{1,0:T(4,128)S(1)},...) while((s32[]{:T(128)}, f32[2,6,2048]{2,1,0:T(8,128)S(1)}, ...), condition=%wide.region_26.27_spmd, body=%wide.region_19.26_spmd.sunk | while | flops 85970952 | bytes 499925 | solution.py:37
  329.9 16.2 fusion.189
  346.4 16.2 fusion.189
  363.3 32.9 %while.83 = (s32[]{:T(128)}, f32[2,6,2048]{2,1,0:T(8,128)S(1)}, f32[3,1024]{1,0:T(4,128)S(1)}, f32[2,6,2048]{2,1,0:T(8,128)S(1)}, f32[3,1024]{1,0:T(4,128)S(1)},...) while((s32[]{:T(128)}, f32[2,6,2048]{2,1,0:T(8,128)S(1)}, ...), condition=%wide.region_35.36_spmd, body=%wide.region_28.35_spmd.sunk | while | flops 85970952 | bytes 499925 | solution.py:37
  363.4 16.2 fusion.191
  379.9 16.2 fusion.191
  396.2 1.4 gather_fusion.1
  397.6 1.9 scatter_fusion.1
  399.8 97.2 %gather_fusion.15 = s32[16384]{0:T(1024)S(1)} fusion(s32[128]{0:T(128)S(1)} %get-tuple-element.733, s32[16384]{0:T(1024)S(1)} %broadcast_clamp_fusion.2), kind=kCustom, calls=%fused_computation.15 | custom fusion | bytes 196608 | tf_op jit(solution)/shard_map/gather | solution.py:84
  497.1 1.4 gather_fusion.10
  509.3 137.8 %all-reduce.11.cloned.1.call-done = f32[6,4096]{1,0:T(8,128)} async-done(((f32[6,4096]{1,0:T(8,128)}), f32[6,4096]{1,0:T(8,128)}) %all-reduce.11.cloned.1.call-update) | async-done | bytes 98320 | tf_op jit(solution)/shard_map/psum | solution.py:96
  647.2 0.9 constant_dynamic-update-slice_fusion.3
  648.1 141.3 %all-reduce.13.cloned.1.call-done = f32[6,4096]{1,0:T(8,128)} async-done(((f32[6,4096]{1,0:T(8,128)}), f32[6,4096]{1,0:T(8,128)}) %all-reduce.13.cloned.1.call-update) | async-done | bytes 98320 | tf_op jit(solution)/shard_map/psum | solution.py:96
  789.5 0.9 constant_dynamic-update-slice_fusion.2
  790.4 141.8 %all-reduce.15.cloned.1.call-done = f32[6,4096]{1,0:T(8,128)} async-done(((f32[6,4096]{1,0:T(8,128)}), f32[6,4096]{1,0:T(8,128)}) %all-reduce.15.cloned.1.call-update) | async-done | bytes 98320 | tf_op jit(solution)/shard_map/psum | solution.py:96
  933.4 1.4 scatter_fusion
  934.9 1.4 scatter_fusion.3
  936.4 1.4 scatter_fusion.2
  937.9 1.4 scatter_fusion.4
  941.9 59.0 %all-gather.3 = f32[128,6,256]{2,1,0:T(8,128)S(1)} all-gather(f32[1,6,256]{2,1,0:T(8,128)S(1)} %maximum_bitcast_fusion.1), channel_id=3, replica_groups=mesh['grp'=8,'dev'=16] {'grp','dev'}, dimensions={0}, use_global_device_ids=true | all-gather | bytes 792576 | tf_op jit(solution)/shard_map/all_gather | solution.py:85
  1000.9 8.4 copy.274
  1009.3 60.2 %gather_fusion.16 = f32[16384,6]{1,0:T(8,128)} fusion(f32[6,32768]{0,1:T(8,128)} %bitcast.633, s32[16384]{0:T(1024)S(1)} %broadcast_clamp_fusion), kind=kCustom, calls=%fused_computation.16 | custom fusion | bytes 851968 | tf_op jit(solution)/shard_map/gather | solution.py:87
  1069.4 6.2 fusion.166
  1075.6 2.2 copy.276
  1077.9 32.8 %while.84 = (s32[]{:T(128)}, f32[2,6,2048]{2,1,0:T(8,128)S(1)}, f32[3,1024]{1,0:T(4,128)S(1)}, f32[2,6,2048]{2,1,0:T(8,128)S(1)}, f32[3,1024]{1,0:T(4,128)S(1)},...) while((s32[]{:T(128)}, f32[2,6,2048]{2,1,0:T(8,128)S(1)}, ...), condition=%wide.region_52.53_spmd, body=%wide.region_45.52_spmd.sunk | while | flops 85970952 | bytes 499925 | solution.py:37
  1078.0 16.2 fusion.193
  1094.4 16.2 fusion.193
  1110.7 2.3 copy.279
  1113.6 34.0 %while.85 = (s32[]{:T(128)}, f32[2,6,2048]{2,1,0:T(8,128)}, f32[3,1024]{1,0:T(4,128)S(1)}, f32[2,6,2048]{2,1,0:T(8,128)S(1)}, f32[3,1024]{1,0:T(4,128)S(1)}, /*i...) while((s32[]{:T(128)}, f32[2,6,2048]{2,1,0:T(8,128)}, f32[3,1024]{1,0:T(4,128)S(1)}, ...), condition=%wide.region_60.61_spmd, body=%wide.region_53.60_spmd.sunk | while | flops 85970952 | bytes 483541 | solution.py:37
  1113.7 16.2 fusion.195
  1130.7 16.2 fusion.195
  1147.9 2.2 copy.282
  1150.1 32.8 %while.86 = (s32[]{:T(128)}, f32[2,6,2048]{2,1,0:T(8,128)S(1)}, f32[3,1024]{1,0:T(4,128)S(1)}, f32[2,6,2048]{2,1,0:T(8,128)S(1)}, f32[3,1024]{1,0:T(4,128)S(1)},...) while((s32[]{:T(128)}, f32[2,6,2048]{2,1,0:T(8,128)S(1)}, ...), condition=%wide.region_69.70_spmd, body=%wide.region_62.69_spmd.sunk | while | flops 85970952 | bytes 499925 | solution.py:37
  1150.2 16.2 fusion.197
  1166.6 16.2 fusion.197
  1183.7 32.8 %while.87 = (s32[]{:T(128)}, f32[2,6,2048]{2,1,0:T(8,128)S(1)}, f32[3,1024]{1,0:T(4,128)S(1)}, f32[2,6,2048]{2,1,0:T(8,128)S(1)}, f32[3,1024]{1,0:T(4,128)S(1)},...) while((s32[]{:T(128)}, f32[2,6,2048]{2,1,0:T(8,128)S(1)}, ...), condition=%wide.region_78.79_spmd, body=%wide.region_71.78_spmd.sunk | while | flops 85970952 | bytes 499925 | solution.py:37
  1183.8 16.2 fusion.199
  1200.2 16.2 fusion.199
  1219.8 66.7 %all-reduce.17.cloned.1.call-done = f32[6,4096]{1,0:T(8,128)} async-done(((f32[6,4096]{1,0:T(8,128)}), f32[6,4096]{1,0:T(8,128)}) %all-reduce.17.cloned.1.call-update) | async-done | bytes 98320 | tf_op jit(solution)/shard_map/psum | solution.py:96
  1287.5 141.8 %all-reduce.19.cloned.1.call-done = f32[6,4096]{1,0:T(8,128)} async-done(((f32[6,4096]{1,0:T(8,128)}), f32[6,4096]{1,0:T(8,128)}) %all-reduce.19.cloned.1.call-update) | async-done | bytes 98320 | tf_op jit(solution)/shard_map/psum | solution.py:96
  1430.3 141.2 %all-reduce.21.cloned.1.call-done = f32[6,4096]{1,0:T(8,128)} async-done(((f32[6,4096]{1,0:T(8,128)}), f32[6,4096]{1,0:T(8,128)}) %all-reduce.21.cloned.1.call-update) | async-done | bytes 98320 | tf_op jit(solution)/shard_map/psum | solution.py:96
  1571.5 0.9 constant_dynamic-update-slice_fusion.7
  1572.5 142.0 %all-reduce.23.cloned.1.call-done = f32[6,4096]{1,0:T(8,128)} async-done(((f32[6,4096]{1,0:T(8,128)}), f32[6,4096]{1,0:T(8,128)}) %all-reduce.23.cloned.1.call-update) | async-done | bytes 98320 | tf_op jit(solution)/shard_map/psum | solution.py:96
  1715.6 1.4 scatter_fusion.5
  1717.9 1.4 scatter_fusion.6
  1720.2 1.4 scatter_fusion.7
  1722.6 1.4 scatter_fusion.8
  (218 shorter events, 34.7 us)
Async XLA Ops:
  7.2 501.2 %all-reduce.9.cloned.1.call-start = ((), (), s32[]{:S(2)}) async-start(), calls=%async_computation | async-start | bytes 262144 | tf_op jit(solution)/shard_map/psum | solution.py:96
  78.7 11.5 copy-start.18
  289.1 0.6 copy-start.5
  289.8 357.4 %all-reduce.11.cloned.1.call-start = ((), (), s32[]{:S(2)}) async-start(), calls=%async_computation.1 | async-start | bytes 262144 | tf_op jit(solution)/shard_map/psum | solution.py:96
  327.5 2.3 copy-start.6
  362.7 0.7 copy-start.7
  396.2 100.8 %copy-start.8 = (f32[2,6,2048]{2,1,0:T(8,128)}, f32[2,6,2048]{2,1,0:T(8,128)S(1)}, u32[]{:S(2)}) copy-start(f32[2,6,2048]{2,1,0:T(8,128)S(1)} %get-tuple-element.238) | copy-start | bytes 294916
  397.6 543.1 %copy-start.15 = (s32[1024]{0:T(1024)}, s32[1024]{0:T(1024)S(1)}, u32[]{:S(2)}) copy-start(s32[1024]{0:T(1024)S(1)} %pad_clamp_fusion) | copy-start | bytes 12292
  399.7 99.4 %copy-start.11 = (f32[3,1024]{1,0:T(4,128)S(1)}, f32[3,1024]{1,0:T(4,128)}, u32[]{:S(2)}) copy-start(f32[3,1024]{1,0:T(4,128)} %param.23) | copy-start | bytes 36868
  399.7 99.6 %copy-start.12 = (f32[3,1024]{1,0:T(4,128)S(1)}, f32[3,1024]{1,0:T(4,128)}, u32[]{:S(2)}) copy-start(f32[3,1024]{1,0:T(4,128)} %param.25) | copy-start | bytes 36868
  399.7 99.8 %copy-start.13 = (f32[3,1024]{1,0:T(4,128)S(1)}, f32[3,1024]{1,0:T(4,128)}, u32[]{:S(2)}) copy-start(f32[3,1024]{1,0:T(4,128)} %param.24) | copy-start | bytes 36868
  399.7 100.7 %copy-start.14 = (f32[3,1024]{1,0:T(4,128)S(1)}, f32[3,1024]{1,0:T(4,128)}, u32[]{:S(2)}) copy-start(f32[3,1024]{1,0:T(4,128)} %param.26) | copy-start | bytes 36868
  508.4 281.0 %all-reduce.13.cloned.1.call-start = ((), (), s32[]{:S(2)}) async-start(), calls=%async_computation.2 | async-start | bytes 262144 | tf_op jit(solution)/shard_map/psum | solution.py:96
  647.2 285.0 %all-reduce.15.cloned.1.call-start = ((), (), s32[]{:S(2)}) async-start(), calls=%async_computation.3 | async-start | bytes 262144 | tf_op jit(solution)/shard_map/psum | solution.py:96
  789.4 497.1 %all-reduce.17.cloned.1.call-start = ((), (), s32[]{:S(2)}) async-start(), calls=%async_computation.4 | async-start | bytes 262144 | tf_op jit(solution)/shard_map/psum | solution.py:96
  934.7 74.5 %copy-start.2 = (f32[3,1024]{0,1:T(8,128)}, f32[3,1024]{0,1:T(8,128)S(1)}, u32[]{:S(2)}) copy-start(f32[3,1024]{0,1:T(8,128)S(1)} %scatter_fusion) | copy-start | bytes 36868
  936.3 73.0 %copy-start = (f32[3,1024]{0,1:T(8,128)}, f32[3,1024]{0,1:T(8,128)S(1)}, u32[]{:S(2)}) copy-start(f32[3,1024]{0,1:T(8,128)S(1)} %scatter_fusion.3) | copy-start | bytes 36868
  1110.7 2.9 copy-start.9
  1147.6 281.7 %all-reduce.19.cloned.1.call-start = ((), (), s32[]{:S(2)}) async-start(), calls=%async_computation.5 | async-start | bytes 262144 | tf_op jit(solution)/shard_map/psum | solution.py:96
  1183.0 0.7 copy-start.10
  1183.6 32.9 %copy-start.1 = (f32[3,1024]{0,1:T(8,128)S(1)}, f32[3,1024]{0,1:T(8,128)}, u32[]{:S(2)}) copy-start(f32[3,1024]{0,1:T(8,128)} %copy-done) | copy-start | bytes 36868
  1183.6 32.9 %copy-start.16 = (s32[1024]{0:T(1024)S(1)}, s32[1024]{0:T(1024)}, u32[]{:S(2)}) copy-start(s32[1024]{0:T(1024)} %copy-done.15) | copy-start | bytes 12292
  1183.6 34.3 %copy-start.3 = (f32[3,1024]{0,1:T(8,128)S(1)}, f32[3,1024]{0,1:T(8,128)}, u32[]{:S(2)}) copy-start(f32[3,1024]{0,1:T(8,128)} %copy-done.2) | copy-start | bytes 36868
  1183.6 531.7 %copy-start.19 = (f32[256]{0:T(256)S(1)}, f32[256]{0:T(256)}, u32[]{:S(2)}) copy-start(f32[256]{0:T(256)} %get-tuple-element.731) | copy-start | bytes 3076
  1183.6 531.7 %copy-start.20 = (f32[256]{0:T(256)S(1)}, f32[256]{0:T(256)}, u32[]{:S(2)}) copy-start(f32[256]{0:T(256)} %get-tuple-element.732) | copy-start | bytes 3076
  1183.7 531.9 %copy-start.17 = (s32[256,1]{0,1:T(1,128)S(1)}, s32[256,1]{0,1:T(1,128)}, u32[]{:S(2)}) copy-start(s32[256,1]{0,1:T(1,128)} %get-tuple-element.729) | copy-start | bytes 3076
  1216.5 355.0 %copy-start.4 = (f32[2,6,2048]{2,1,0:T(8,128)}, f32[2,6,2048]{2,1,0:T(8,128)S(1)}, u32[]{:S(2)}) copy-start(f32[2,6,2048]{2,1,0:T(8,128)S(1)} %get-tuple-element.248) | copy-start | bytes 294916
  1286.5 285.0 %all-reduce.21.cloned.1.call-start = ((), (), s32[]{:S(2)}) async-start(), calls=%async_computation.6 | async-start | bytes 262144 | tf_op jit(solution)/shard_map/psum | solution.py:96
  1429.3 285.1 %all-reduce.23.cloned.1.call-start = ((), (), s32[]{:S(2)}) async-start(), calls=%async_computation.7 | async-start | bytes 262144 | tf_op jit(solution)/shard_map/psum | solution.py:96
Sparse Core Ops, SparseCore 0:
  289.9 138.5 all-reduce.8
  508.5 138.5 all-reduce.10
  651.9 137.4 all-reduce.12
  794.7 137.4 all-reduce.14
  1147.8 138.6 all-reduce.16
  1291.8 137.4 all-reduce.18
  1434.0 137.4 all-reduce.20
  1577.0 137.4 all-reduce.22
where the time goes:
time: 1740 us; the launch traced here: 1730 us
  waiting for transfers between devices  913 us (52%)
  local copies, waits for them, and re-layouts  405 us (23%)
  other arithmetic  270 us (16%)
  blocking collectives  123 us (7%)
  between operations  19 us (1%)
    psum x8, waiting for transfers between devices, shards(): summed = lax.psum(terms, ('grp', 'dev'))  913 us
    reduce_sum x16, other arithmetic, pair_block(): jnp.sum(weight * (drift_z - along * gap_z), axis=1)  259 us
    gather x2, local copies, waits for them, and re-layouts, shards(): slot = owner * slot_cap + place - first[owner]  194 us
    all_gather x2, blocking collectives, shards(): gathered = lax.all_gather(targets[None], ('grp', 'dev'), axis=0, tiled=True)  123 us
    gather x2, local copies, waits for them, and re-layouts, shards(): compact = flat[:, slot]  120 us
  transfers between devices with their start and end apart: 8, of which 7 were waited for; matrix products, arithmetic and copies ran while one was open for 17% of the time, Pallas kernels for 0%

commit v1 on v0

--- a/solution.py
+++ b/solution.py
@@ -82,7 +82,12 @@
         owner = jnp.sum((inclusive[None, :] <= place[:, None]).astype(jnp.int32), axis=1)
         owner = jnp.minimum(owner, devices_all - 1)
         slot = owner * slot_cap + place - first[owner]
-        gathered = lax.all_gather(targets[None], ("grp", "dev"), axis=0, tiled=True)
+        gathered = jnp.concatenate(
+            lax.all_to_all(
+                jnp.stack([targets[None]] * lax.axis_size(("grp", "dev"))), ("grp", "dev"), 0, 0
+            ),
+            axis=0,
+        )
         flat = gathered.transpose(1, 0, 2).reshape(6, devices_all * slot_cap)
         compact = flat[:, slot]
         parts = []

time: 1740 us -> 1750 us (level)
  blocking collectives: 123 us -> 0 us
  waiting for transfers between devices: 913 us -> 988 us
  local copies, waits for them, and re-layouts: 405 us -> 431 us
  starting transfers between devices: 0.82 us -> 18.4 us
    all_gather x2 -> x0, blocking collectives: 123 us -> none  [shards(): gathered = lax.all_gather(targets[None], ('grp', 'dev'), axis=0, tiled=True)]
    psum x8, waiting for transfers between devices: 913 us -> 985 us  [shards(): summed = lax.psum(terms, ('grp', 'dev'))]
  transfers between devices with their start and end apart: 8 -> 10, of which waited for: 7 -> 9; matrix products, arithmetic and copies ran while one was open for 17% -> 22% of each run, Pallas kernels for 0% -> 0%
where the time goes in v1:
time: 1750 us; the launch traced here: 1740 us
  waiting for transfers between devices  988 us (56%)
  local copies, waits for them, and re-layouts  431 us (25%)
  other arithmetic  280 us (16%)
  between operations  19.2 us (1%)
  starting transfers between devices  18.4 us (1%)
    psum x8, waiting for transfers between devices, shards(): summed = lax.psum(terms, ('grp', 'dev'))  985 us
    reduce_sum x16, other arithmetic, pair_block(): jnp.sum(weight * (drift_z - along * gap_z), axis=1)  266 us
    gather x2, local copies, waits for them, and re-layouts, shards(): slot = owner * slot_cap + place - first[owner]  194 us
    gather x2, local copies, waits for them, and re-layouts, shards(): compact = flat[:, slot]  120 us
  transfers between devices with their start and end apart: 10, of which 9 were waited for; matrix products, arithmetic and copies ran while one was open for 22% of the time, Pallas kernels for 0%

profile of v1, /device:TPU:1, one launch (start us, length us, event | category | flops | bytes accessed | tf_op | source)
XLA Modules:
  0.0 1737.8 jit_solution(6084078195157226343)
XLA Ops:
  8.5 2.6 compare_select_fusion.4
  16.0 11.5 all-to-all-start
  32.2 2.3 convert_reduce_fusion.1
  35.3 2.3 convert_reduce_fusion
  42.5 97.2 %gather_fusion.6 = s32[16384]{0:T(1024)S(1)} fusion(s32[128]{0:T(128)S(1)} %get-tuple-element.778, s32[16384]{0:T(1024)S(1)} %broadcast_clamp_fusion.3), kind=kCustom, calls=%fused_computation.6 | custom fusion | bytes 196608 | tf_op jit(solution)/shard_map/gather | solution.py:84
  141.2 1.4 gather_fusion.1
  145.3 1.7 scatter_fusion.1
  147.0 97.2 %gather_fusion.15 = s32[16384]{0:T(1024)S(1)} fusion(s32[128]{0:T(128)S(1)} %get-tuple-element.777, s32[16384]{0:T(1024)S(1)} %broadcast_clamp_fusion.2), kind=kCustom, calls=%fused_computation.15 | custom fusion | bytes 196608 | tf_op jit(solution)/shard_map/gather | solution.py:84
  245.5 8.7 copy.361
  254.1 60.2 %gather_fusion.7 = f32[16384,6]{1,0:T(8,128)} fusion(f32[6,32768]{0,1:T(8,128)} %bitcast.634, s32[16384]{0:T(1024)S(1)} %broadcast_clamp_fusion.1), kind=kCustom, calls=%fused_computation.7 | custom fusion | bytes 851968 | tf_op jit(solution)/shard_map/gather | solution.py:92
  314.3 6.2 fusion.167
  320.5 2.2 copy.318
  323.4 36.6 %while.80 = (s32[]{:T(128)}, f32[2,6,2048]{2,1,0:T(8,128)}, f32[3,1024]{1,0:T(4,128)S(1)}, f32[2,6,2048]{2,1,0:T(8,128)S(1)}, f32[3,1024]{1,0:T(4,128)S(1)}, /*i...) while((s32[]{:T(128)}, f32[2,6,2048]{2,1,0:T(8,128)}, f32[3,1024]{1,0:T(4,128)S(1)}, ...), condition=%wide.region_9.10_spmd, body=%wide.region_2.9_spmd.sunk | while | flops 85970952 | bytes 483541 | solution.py:37
  323.5 16.8 fusion.185
  341.8 16.8 fusion.185
  360.0 2.2 copy.319
  362.9 36.6 %while.81 = (s32[]{:T(128)}, f32[2,6,2048]{2,1,0:T(8,128)}, f32[3,1024]{1,0:T(4,128)S(1)}, f32[2,6,2048]{2,1,0:T(8,128)S(1)}, f32[3,1024]{1,0:T(4,128)S(1)}, /*i...) while((s32[]{:T(128)}, f32[2,6,2048]{2,1,0:T(8,128)}, f32[3,1024]{1,0:T(4,128)S(1)}, ...), condition=%wide.region_17.18_spmd, body=%wide.region_10.17_spmd.sunk | while | flops 85970952 | bytes 483541 | solution.py:37
  363.0 16.8 fusion.187
  381.3 16.8 fusion.187
  400.1 2.2 copy.320
  403.0 36.6 %while.82 = (s32[]{:T(128)}, f32[2,6,2048]{2,1,0:T(8,128)}, f32[3,1024]{1,0:T(4,128)S(1)}, f32[2,6,2048]{2,1,0:T(8,128)S(1)}, f32[3,1024]{1,0:T(4,128)S(1)}, /*i...) while((s32[]{:T(128)}, f32[2,6,2048]{2,1,0:T(8,128)}, f32[3,1024]{1,0:T(4,128)S(1)}, ...), condition=%wide.region_26.27_spmd, body=%wide.region_19.26_spmd.sunk | while | flops 85970952 | bytes 483541 | solution.py:37
  403.1 16.8 fusion.189
  421.4 16.8 fusion.189
  440.4 32.8 %while.83 = (s32[]{:T(128)}, f32[2,6,2048]{2,1,0:T(8,128)S(1)}, f32[3,1024]{1,0:T(4,128)S(1)}, f32[2,6,2048]{2,1,0:T(8,128)S(1)}, f32[3,1024]{1,0:T(4,128)S(1)},...) while((s32[]{:T(128)}, f32[2,6,2048]{2,1,0:T(8,128)S(1)}, ...), condition=%wide.region_35.36_spmd, body=%wide.region_28.35_spmd.sunk | while | flops 85970952 | bytes 499925 | solution.py:37
  440.5 16.2 fusion.191
  456.9 16.2 fusion.191
  473.2 68.0 %all-reduce.9.cloned.1.call-done = f32[6,4096]{1,0:T(8,128)} async-done(((f32[6,4096]{1,0:T(8,128)}), f32[6,4096]{1,0:T(8,128)}) %all-reduce.9.cloned.1.call-update) | async-done | bytes 98320 | tf_op jit(solution)/shard_map/psum | solution.py:101
  542.2 142.0 %all-reduce.11.cloned.1.call-done = f32[6,4096]{1,0:T(8,128)} async-done(((f32[6,4096]{1,0:T(8,128)}), f32[6,4096]{1,0:T(8,128)}) %all-reduce.11.cloned.1.call-update) | async-done | bytes 98320 | tf_op jit(solution)/shard_map/psum | solution.py:101
  685.2 141.3 %all-reduce.13.cloned.1.call-done = f32[6,4096]{1,0:T(8,128)} async-done(((f32[6,4096]{1,0:T(8,128)}), f32[6,4096]{1,0:T(8,128)}) %all-reduce.13.cloned.1.call-update) | async-done | bytes 98320 | tf_op jit(solution)/shard_map/psum | solution.py:101
  827.4 141.9 %all-reduce.15.cloned.1.call-done = f32[6,4096]{1,0:T(8,128)} async-done(((f32[6,4096]{1,0:T(8,128)}), f32[6,4096]{1,0:T(8,128)}) %all-reduce.15.cloned.1.call-update) | async-done | bytes 98320 | tf_op jit(solution)/shard_map/psum | solution.py:101
  970.5 1.4 scatter_fusion
  972.0 1.4 scatter_fusion.3
  973.6 1.4 scatter_fusion.2
  975.1 1.4 scatter_fusion.4
  978.7 1.3 stack.175
  980.0 5.7 all-to-all-start.1
  987.9 1.4 gather_fusion.10
  998.6 3.6 all-to-all-done.1
  1002.2 8.7 copy.362
  1010.9 60.2 %gather_fusion.16 = f32[16384,6]{1,0:T(8,128)} fusion(f32[6,32768]{0,1:T(8,128)} %bitcast.635, s32[16384]{0:T(1024)S(1)} %broadcast_clamp_fusion), kind=kCustom, calls=%fused_computation.16 | custom fusion | bytes 851968 | tf_op jit(solution)/shard_map/gather | solution.py:92
  1071.1 6.2 fusion.166
  1077.2 2.2 copy.340
  1079.5 35.4 %while.84 = (s32[]{:T(128)}, f32[2,6,2048]{2,1,0:T(8,128)S(1)}, f32[3,1024]{1,0:T(4,128)S(1)}, f32[2,6,2048]{2,1,0:T(8,128)S(1)}, f32[3,1024]{1,0:T(4,128)S(1)},...) while((s32[]{:T(128)}, f32[2,6,2048]{2,1,0:T(8,128)S(1)}, ...), condition=%wide.region_52.53_spmd, body=%wide.region_45.52_spmd.sunk | while | flops 85970952 | bytes 499925 | solution.py:37
  1079.6 16.8 fusion.193
  1097.3 16.8 fusion.193
  1114.9 2.3 copy.343
  1117.8 36.5 %while.85 = (s32[]{:T(128)}, f32[2,6,2048]{2,1,0:T(8,128)}, f32[3,1024]{1,0:T(4,128)S(1)}, f32[2,6,2048]{2,1,0:T(8,128)S(1)}, f32[3,1024]{1,0:T(4,128)S(1)}, /*i...) while((s32[]{:T(128)}, f32[2,6,2048]{2,1,0:T(8,128)}, f32[3,1024]{1,0:T(4,128)S(1)}, ...), condition=%wide.region_60.61_spmd, body=%wide.region_53.60_spmd.sunk | while | flops 85970952 | bytes 483541 | solution.py:37
  1117.9 16.8 fusion.195
  1136.2 16.8 fusion.195
  1154.6 2.2 copy.346
  1156.9 35.4 %while.86 = (s32[]{:T(128)}, f32[2,6,2048]{2,1,0:T(8,128)S(1)}, f32[3,1024]{1,0:T(4,128)S(1)}, f32[2,6,2048]{2,1,0:T(8,128)S(1)}, f32[3,1024]{1,0:T(4,128)S(1)},...) while((s32[]{:T(128)}, f32[2,6,2048]{2,1,0:T(8,128)S(1)}, ...), condition=%wide.region_69.70_spmd, body=%wide.region_62.69_spmd.sunk | while | flops 85970952 | bytes 499925 | solution.py:37
  1157.0 16.8 fusion.197
  1174.7 16.8 fusion.197
  1193.0 32.9 %while.87 = (s32[]{:T(128)}, f32[2,6,2048]{2,1,0:T(8,128)S(1)}, f32[3,1024]{1,0:T(4,128)S(1)}, f32[2,6,2048]{2,1,0:T(8,128)S(1)}, f32[3,1024]{1,0:T(4,128)S(1)},...) while((s32[]{:T(128)}, f32[2,6,2048]{2,1,0:T(8,128)S(1)}, ...), condition=%wide.region_78.79_spmd, body=%wide.region_71.78_spmd.sunk | while | flops 85970952 | bytes 499925 | solution.py:37
  1193.1 16.2 fusion.199
  1209.5 16.2 fusion.199
  1225.9 66.6 %all-reduce.17.cloned.1.call-done = f32[6,4096]{1,0:T(8,128)} async-done(((f32[6,4096]{1,0:T(8,128)}), f32[6,4096]{1,0:T(8,128)}) %all-reduce.17.cloned.1.call-update) | async-done | bytes 98320 | tf_op jit(solution)/shard_map/psum | solution.py:101
  1293.4 141.8 %all-reduce.19.cloned.1.call-done = f32[6,4096]{1,0:T(8,128)} async-done(((f32[6,4096]{1,0:T(8,128)}), f32[6,4096]{1,0:T(8,128)}) %all-reduce.19.cloned.1.call-update) | async-done | bytes 98320 | tf_op jit(solution)/shard_map/psum | solution.py:101
  1436.2 141.2 %all-reduce.21.cloned.1.call-done = f32[6,4096]{1,0:T(8,128)} async-done(((f32[6,4096]{1,0:T(8,128)}), f32[6,4096]{1,0:T(8,128)}) %all-reduce.21.cloned.1.call-update) | async-done | bytes 98320 | tf_op jit(solution)/shard_map/psum | solution.py:101
  1578.4 142.0 %all-reduce.23.cloned.1.call-done = f32[6,4096]{1,0:T(8,128)} async-done(((f32[6,4096]{1,0:T(8,128)}), f32[6,4096]{1,0:T(8,128)}) %all-reduce.23.cloned.1.call-update) | async-done | bytes 98320 | tf_op jit(solution)/shard_map/psum | solution.py:101
  1721.6 1.4 scatter_fusion.5
  1723.9 1.4 scatter_fusion.6
  1726.3 1.4 scatter_fusion.7
  1728.6 1.4 scatter_fusion.8
  (246 shorter events, 64.6 us)
Async XLA Ops:
  11.1 134.2 %copy-start.14 = (s32[256,1]{0,1:T(1,128)}, s32[256,1]{0,1:T(1,128)S(1)}, u32[]{:S(2)}) copy-start(s32[256,1]{0,1:T(1,128)S(1)} %get-tuple-element.774) | copy-start | bytes 3076
  16.0 229.4 %all-to-all-start = ((f32[128,1,6,256]{3,1,2,0:T(1,128)}), f32[128,1,6,256]{3,1,2,0:T(1,128)S(1)}, u32[]{:S(2)}, u32[]{:S(2)}) async-start(f32[128,1,6,256]{3,1,2,0:T(1,128)} %stack.174), calls=%async_computation | async-start | bytes 1572864 | tf_op jit(solution)/shard_map/all_to_all | solution.py:86
  27.5 513.7 %all-reduce.9.cloned.1.call-start = ((), (), s32[]{:S(2)}) async-start(), calls=%async_computation.2 | async-start | bytes 262144 | tf_op jit(solution)/shard_map/psum | solution.py:101
  28.5 111.2 %copy-start.4 = (f32[3,1024]{0,1:T(8,128)}, f32[3,1024]{0,1:T(8,128)S(1)}, u32[]{:S(2)}) copy-start(f32[3,1024]{0,1:T(8,128)S(1)} %copy.324) | copy-start | bytes 36868
  29.5 110.3 %copy-start = (f32[3,1024]{0,1:T(8,128)}, f32[3,1024]{0,1:T(8,128)S(1)}, u32[]{:S(2)}) copy-start(f32[3,1024]{0,1:T(8,128)S(1)} %copy.309) | copy-start | bytes 36868
  399.5 284.7 %all-reduce.11.cloned.1.call-start = ((), (), s32[]{:S(2)}) async-start(), calls=%async_computation.3 | async-start | bytes 262144 | tf_op jit(solution)/shard_map/psum | solution.py:101
  440.2 529.9 %copy-start.21 = (f32[256,3]{0,1:T(4,128)S(1)}, f32[256,3]{0,1:T(4,128)}, u32[]{:S(2)}) copy-start(f32[256,3]{0,1:T(4,128)} %copy.310) | copy-start | bytes 9220
  440.3 529.9 %copy-start.22 = (f32[256,3]{0,1:T(4,128)S(1)}, f32[256,3]{0,1:T(4,128)}, u32[]{:S(2)}) copy-start(f32[256,3]{0,1:T(4,128)} %copy.308) | copy-start | bytes 9220
  440.3 529.9 %copy-start.23 = (f32[256,3]{0,1:T(4,128)S(1)}, f32[256,3]{0,1:T(4,128)}, u32[]{:S(2)}) copy-start(f32[256,3]{0,1:T(4,128)} %copy.306) | copy-start | bytes 9220
  440.3 529.9 %copy-start.24 = (f32[256,3]{0,1:T(4,128)S(1)}, f32[256,3]{0,1:T(4,128)}, u32[]{:S(2)}) copy-start(f32[256,3]{0,1:T(4,128)} %copy.323) | copy-start | bytes 9220
  440.3 529.9 %copy-start.29 = (f32[256]{0:T(256)S(1)}, f32[256]{0:T(256)}, u32[]{:S(2)}) copy-start(f32[256]{0:T(256)} %get-tuple-element.783) | copy-start | bytes 3076
  440.3 529.9 %copy-start.30 = (f32[256]{0:T(256)S(1)}, f32[256]{0:T(256)}, u32[]{:S(2)}) copy-start(f32[256]{0:T(256)} %get-tuple-element.784) | copy-start | bytes 3076
  440.3 530.2 %copy-start.5 = (f32[3,1024]{0,1:T(8,128)S(1)}, f32[3,1024]{0,1:T(8,128)}, u32[]{:S(2)}) copy-start(f32[3,1024]{0,1:T(8,128)} %copy-done.4) | copy-start | bytes 36868
  440.3 530.2 %copy-start.15 = (s32[256,1]{0,1:T(1,128)S(1)}, s32[256,1]{0,1:T(1,128)}, u32[]{:S(2)}) copy-start(s32[256,1]{0,1:T(1,128)} %copy-done.14) | copy-start | bytes 3076
  440.3 531.7 %copy-start.1 = (f32[3,1024]{0,1:T(8,128)S(1)}, f32[3,1024]{0,1:T(8,128)}, u32[]{:S(2)}) copy-start(f32[3,1024]{0,1:T(8,128)} %copy-done) | copy-start | bytes 36868
  440.3 536.1 %copy-start.18 = (f32[1024]{0:T(1024)S(1)}, f32[1024]{0:T(1024)}, u32[]{:S(2)}) copy-start(f32[1024]{0:T(1024)} %get-tuple-element.764) | copy-start | bytes 12292
  440.4 536.1 %copy-start.19 = (f32[1024]{0:T(1024)S(1)}, f32[1024]{0:T(1024)}, u32[]{:S(2)}) copy-start(f32[1024]{0:T(1024)} %get-tuple-element.765) | copy-start | bytes 12292
  440.4 536.1 %copy-start.20 = (f32[1024]{0:T(1024)S(1)}, f32[1024]{0:T(1024)}, u32[]{:S(2)}) copy-start(f32[1024]{0:T(1024)} %get-tuple-element.766) | copy-start | bytes 12292
  440.4 536.6 %copy-start.16 = (s32[1024]{0:T(1024)S(1)}, s32[1024]{0:T(1024)}, u32[]{:S(2)}) copy-start(s32[1024]{0:T(1024)} %pad_clamp_fusion) | copy-start | bytes 12292
  473.2 353.2 %copy-start.11 = (f32[2,6,2048]{2,1,0:T(8,128)}, f32[2,6,2048]{2,1,0:T(8,128)S(1)}, u32[]{:S(2)}) copy-start(f32[2,6,2048]{2,1,0:T(8,128)S(1)} %get-tuple-element.238) | copy-start | bytes 294916
  541.3 285.2 %all-reduce.13.cloned.1.call-start = ((), (), s32[]{:S(2)}) async-start(), calls=%async_computation.4 | async-start | bytes 262144 | tf_op jit(solution)/shard_map/psum | solution.py:101
  684.2 285.0 %all-reduce.15.cloned.1.call-start = ((), (), s32[]{:S(2)}) async-start(), calls=%async_computation.5 | async-start | bytes 262144 | tf_op jit(solution)/shard_map/psum | solution.py:101
  971.9 39.0 %copy-start.6 = (f32[3,1024]{0,1:T(8,128)}, f32[3,1024]{0,1:T(8,128)S(1)}, u32[]{:S(2)}) copy-start(f32[3,1024]{0,1:T(8,128)S(1)} %scatter_fusion) | copy-start | bytes 36868
  973.4 37.5 %copy-start.2 = (f32[3,1024]{0,1:T(8,128)}, f32[3,1024]{0,1:T(8,128)S(1)}, u32[]{:S(2)}) copy-start(f32[3,1024]{0,1:T(8,128)S(1)} %scatter_fusion.3) | copy-start | bytes 36868
  977.0 3.0 copy-start.8
  977.0 3.0 copy-start.9
  980.0 22.2 %all-to-all-start.1 = ((f32[128,1,6,256]{3,1,2,0:T(1,128)}), f32[128,1,6,256]{3,1,2,0:T(1,128)S(1)}, u32[]{:S(2)}, u32[]{:S(2)}) async-start(f32[128,1,6,256]{3,1,2,0:T(1,128)} %stack.175), calls=%async_computation.1 | async-start | bytes 1572864 | tf_op jit(solution)/shard_map/all_to_all | solution.py:86
  985.6 306.8 %all-reduce.17.cloned.1.call-start = ((), (), s32[]{:S(2)}) async-start(), calls=%async_computation.6 | async-start | bytes 262144 | tf_op jit(solution)/shard_map/psum | solution.py:101
  1114.9 2.9 copy-start.12
  1154.4 280.9 %all-reduce.19.cloned.1.call-start = ((), (), s32[]{:S(2)}) async-start(), calls=%async_computation.7 | async-start | bytes 262144 | tf_op jit(solution)/shard_map/psum | solution.py:101
  1192.2 0.8 copy-start.13
  1192.9 528.4 %copy-start.25 = (f32[256,3]{0,1:T(4,128)S(1)}, f32[256,3]{0,1:T(4,128)}, u32[]{:S(2)}) copy-start(f32[256,3]{0,1:T(4,128)} %copy.332) | copy-start | bytes 9220
  1192.9 528.4 %copy-start.26 = (f32[256,3]{0,1:T(4,128)S(1)}, f32[256,3]{0,1:T(4,128)}, u32[]{:S(2)}) copy-start(f32[256,3]{0,1:T(4,128)} %copy.329) | copy-start | bytes 9220
  1192.9 528.4 %copy-start.27 = (f32[256,3]{0,1:T(4,128)S(1)}, f32[256,3]{0,1:T(4,128)}, u32[]{:S(2)}) copy-start(f32[256,3]{0,1:T(4,128)} %copy.326) | copy-start | bytes 9220
  1192.9 528.4 %copy-start.28 = (f32[256,3]{0,1:T(4,128)S(1)}, f32[256,3]{0,1:T(4,128)}, u32[]{:S(2)}) copy-start(f32[256,3]{0,1:T(4,128)} %copy.352) | copy-start | bytes 9220
  1193.0 528.4 %copy-start.31 = (f32[256]{0:T(256)S(1)}, f32[256]{0:T(256)}, u32[]{:S(2)}) copy-start(f32[256]{0:T(256)} %get-tuple-element.775) | copy-start | bytes 3076
  1193.0 528.4 %copy-start.32 = (f32[256]{0:T(256)S(1)}, f32[256]{0:T(256)}, u32[]{:S(2)}) copy-start(f32[256]{0:T(256)} %get-tuple-element.776) | copy-start | bytes 3076
  1193.0 528.6 %copy-start.7 = (f32[3,1024]{0,1:T(8,128)S(1)}, f32[3,1024]{0,1:T(8,128)}, u32[]{:S(2)}) copy-start(f32[3,1024]{0,1:T(8,128)} %copy-done.6) | copy-start | bytes 36868
  1193.0 528.6 %copy-start.17 = (s32[256,1]{0,1:T(1,128)S(1)}, s32[256,1]{0,1:T(1,128)}, u32[]{:S(2)}) copy-start(s32[256,1]{0,1:T(1,128)} %get-tuple-element.773) | copy-start | bytes 3076
  1193.0 533.3 %copy-start.3 = (f32[3,1024]{0,1:T(8,128)S(1)}, f32[3,1024]{0,1:T(8,128)}, u32[]{:S(2)}) copy-start(f32[3,1024]{0,1:T(8,128)} %copy-done.2) | copy-start | bytes 36868
  1225.9 351.6 %copy-start.10 = (f32[2,6,2048]{2,1,0:T(8,128)}, f32[2,6,2048]{2,1,0:T(8,128)S(1)}, u32[]{:S(2)}) copy-start(f32[2,6,2048]{2,1,0:T(8,128)S(1)} %get-tuple-element.248) | copy-start | bytes 294916
  1292.5 285.0 %all-reduce.21.cloned.1.call-start = ((), (), s32[]{:S(2)}) async-start(), calls=%async_computation.8 | async-start | bytes 262144 | tf_op jit(solution)/shard_map/psum | solution.py:101
  1435.3 285.1 %all-reduce.23.cloned.1.call-start = ((), (), s32[]{:S(2)}) async-start(), calls=%async_computation.9 | async-start | bytes 262144 | tf_op jit(solution)/shard_map/psum | solution.py:101
Sparse Core Ops, SparseCore 0:
  399.6 141.5 all-reduce.8
  546.7 137.4 all-reduce.10
  688.9 137.4 all-reduce.12
  831.8 137.4 all-reduce.14
  1154.5 137.9 all-reduce.16
  1297.8 137.4 all-reduce.18
  1440.0 137.4 all-reduce.20
  1582.9 137.4 all-reduce.22
